TPU v7x, 32 devices: a whole 2x2x4 slice. The times are simulated.
32 devices in a mesh: snp: 8 (over z, y), ind: 4 (over x, core).
Axes of the slice: x: 2, y: 2, z: 4, core: 2. Of those that a mesh axis runs over, the one named last changes fastest.
Arguments:
- beta_hat: float32 [64, 8192], P('ind', 'snp'), may hold values from -8 to 8
- ld_band: float32 [8192, 1024], P('snp'), as said below
- band_start: int32 [64], P('snp'), may hold values from -480 to 7648, as said below
- heritability: float32 [64], P('ind'), may hold values from 0.2 to 0.6
- genotypes: bfloat16 [4096, 8192], P('ind', 'snp'), may hold values from 0 to 2, as said below
Outputs:
- weights: float32 [64, 8192], P('ind', 'snp')
- scores: float32 [64, 4096], P(None, ('ind', 'snp'))
Inputs may be any that keep to these rules, and one draw needn't show every extreme that they name: ld_band is a symmetric matrix R in band form: entry k of row i is R[i, band_start[i // 128] + k]; R[i, i] = 1; R[i, j] = 0 when |i - j| > 416 or j lies outside the SNPs; the off-diagonal magnitudes of a row sum to 2.5 at most. `band_start`: block b's window starts at 128 * b - 416 - k with k from 0 to 64; the first block has k = 64 and the last block k = 0. `genotypes`: dosages are 0, 1 or 2.
All inputs are finite; a program needn't handle non-finite values.
Results may differ from a plain program's by a relative error of at most 0.0021.
Values may be sent and summed in bfloat16 or wider, within the bound.
No kernel may reach another device: no remote copies, remote signals or barrier semaphores. Data moves between devices by JAX's collectives and lax.ppermute only.
A program may use at most 64 MiB of HBM per device.

v0:
```python
import jax
import jax.numpy as jnp
from jax import lax
from jax.sharding import PartitionSpec as P

BLK = 128
ITERS = 2
M_GENOME = 1100000
N_GWAS = 1000000
REACH = 416
SHIFT_BITS = 7


def all_sum(x, axes, count):
    sent = jnp.broadcast_to(x[None], (count,) + x.shape)
    return jnp.sum(lax.all_to_all(sent, axes, 0, 0, tiled=True), axis=0)


def with_halo(block, width):
    count = lax.axis_size("snp")
    forward = [(i, i + 1) for i in range(count - 1)]
    backward = [(target, source) for source, target in forward]
    low = lax.ppermute(block[:, block.shape[1] - width :], "snp", forward)
    high = lax.ppermute(block[:, :width], "snp", backward)
    return jnp.concatenate([low, block, high], axis=1)


def apply_operator(vector, ld_band, shifts, ridge_shift, halo):
    band_cols = ld_band.shape[1]
    blocks_here = ld_band.shape[0] // BLK
    span = band_cols + (1 << SHIFT_BITS) - 1
    padded = with_halo(vector, halo)
    need = (blocks_here - 1) * BLK + span
    padded = jnp.pad(padded, ((0, 0), (0, max(0, need - padded.shape[1]))))
    wide = jnp.stack([padded[:, b * BLK : b * BLK + span] for b in range(blocks_here)])
    for bit in range(SHIFT_BITS):
        step = 1 << bit
        take = (shifts >> bit & 1)[:, None, None] == 1
        wide = jnp.where(take, wide[:, :, step:], wide[:, :, :-step])
    windows = wide[:, :, :band_cols]
    blocks = ld_band.reshape(blocks_here, BLK, band_cols)
    product = jnp.einsum("btk,brk->tbr", windows, blocks, precision=lax.Precision.HIGHEST)
    return product.reshape(vector.shape) + ridge_shift[:, None] * vector


def local(beta_hat, ld_band, band_start, heritability, genotypes):
    n_snp = lax.axis_size("snp")
    n_ind = lax.axis_size("ind")
    n_all = n_snp * n_ind
    me_ind = lax.axis_index("ind")
    traits_here, rows_here = beta_hat.shape
    traits = traits_here * n_ind
    halo = ld_band.shape[1] - BLK - REACH
    offsets = band_start - lax.axis_index("snp") * rows_here + halo
    shifts = offsets - jnp.arange(band_start.shape[0], dtype=jnp.int32) * BLK
    ridge_shift = M_GENOME / N_GWAS / heritability
    colsum = jnp.sum(genotypes.astype(jnp.float32), axis=0)
    colsum = all_sum(colsum, "ind", n_ind)
    beta_all = lax.all_gather(beta_hat, "ind", axis=0, tiled=True)
    image = apply_operator(beta_hat, ld_band, shifts, ridge_shift, halo)
    image_all = lax.all_gather(image, "ind", axis=0, tiled=True)
    image2 = apply_operator(image, ld_band, shifts, ridge_shift, halo)
    moments = jnp.stack(
        [
            jnp.sum(beta_hat * beta_hat, axis=1),
            jnp.sum(beta_hat * image, axis=1),
            jnp.sum(image * image, axis=1),
            jnp.sum(image * image2, axis=1),
        ]
    )
    placed = jnp.zeros((4, traits), jnp.float32)
    placed = lax.dynamic_update_slice_in_dim(placed, moments, me_ind * traits_here, 1)
    m0, m1, m2, m3 = all_sum(placed, ("ind", "snp"), n_all)
    alpha1 = m0 / m1
    norm1 = alpha1 * alpha1 * m2 - m0
    ratio = norm1 / m0
    grow = 1.0 + ratio
    curv = grow * grow * m1 - 2.0 * grow * alpha1 * m2 + alpha1 * alpha1 * m3
    alpha2 = norm1 / curv
    residual = beta_all - alpha1[:, None] * image_all
    direction = residual + ratio[:, None] * beta_all
    weights_all = alpha1[:, None] * beta_all + alpha2[:, None] * direction
    weights = lax.dynamic_slice_in_dim(weights_all, me_ind * traits_here, traits_here, 0)
    rounded = weights_all.astype(jnp.bfloat16)
    partial = lax.dot_general(
        rounded, genotypes, (((1,), (1,)), ((), ())), preferred_element_type=jnp.float32
    )
    mean_part = jnp.sum(rounded.astype(jnp.float32) * colsum[None, :], axis=1)
    inds_here = genotypes.shape[0]
    share = inds_here // n_snp
    chunks = partial.reshape(traits, n_snp, share).transpose(1, 0, 2).reshape(n_snp, traits * share)
    extra = jnp.broadcast_to(
        jnp.pad(mean_part, (0, 128 - traits % 128 if traits % 128 else 0))[None],
        (n_snp, -(-traits // 128) * 128),
    )
    sent = jnp.concatenate([chunks, extra], axis=1).reshape(n_snp, -1, 128)
    got = jnp.sum(lax.all_to_all(sent, "snp", 0, 0, tiled=True), axis=0).reshape(-1)
    complete = got[: traits * share].reshape(traits, share)
    count = inds_here * n_ind
    average = got[traits * share : traits * share + traits] / count
    centred = complete - average[:, None]
    variance = all_sum(jnp.sum(centred * centred, axis=1), ("ind", "snp"), n_all) / count
    scores = centred * lax.rsqrt(variance + 1e-05)[:, None]
    return (weights, scores)


def solution(mesh):
    placed = (P("ind", "snp"), P("snp", None), P("snp"), P("ind"), P("ind", "snp"))
    return jax.shard_map(
        local,
        mesh=mesh,
        in_specs=placed,
        out_specs=(P("ind", "snp"), P(None, ("ind", "snp"))),
        check_vma=False,
    )
```

profile of v0, /device:TPU:0, one launch (start us, length us, event | category | flops | bytes accessed | tf_op | source)
XLA Modules:
  0.0 93.5 jit_solution(7003058788836734256)
XLA Ops:
  0.6 0.9 fusion.46
  1.5 4.9 %collective-permute-start = (f32[16,480]{1,0:T(8,128)S(1)}, f32[16,480]{1,0:T(8,128)S(1)}, u32[]{:S(2)}, u32[]{:S(2)}) collective-permute-start(f32[16,480]{1,0:T(8,128)S(1)} %get-tuple-element.16), channel_id=1, source_target_pairs={{0,4},{4,8},{8,12},{12,16},{16,20},{20,24},{24,28},{1,5},{5,9},{9,... | collective-permute-start | bytes 92168 | tf_op jit(solution)/shard_map/ppermute | solution.py:23
  6.4 1.3 %collective-permute-start.1 = (f32[16,480]{1,0:T(8,128)S(1)}, f32[16,480]{1,0:T(8,128)S(1)}, u32[]{:S(2)}, u32[]{:S(2)}) collective-permute-start(f32[16,480]{1,0:T(8,128)S(1)} %get-tuple-element.15), channel_id=1, source_target_pairs={{4,0},{8,4},{12,8},{16,12},{20,16},{24,20},{28,24},{5,1},{9,5},{13... | collective-permute-start | bytes 92168 | tf_op jit(solution)/shard_map/ppermute | solution.py:24
  7.7 2.0 %convert_reduce_fusion = f32[1024]{0:T(1024)S(1)} fusion(bf16[1024,1024]{1,0:T(8,128)(2,1)} %param.9), kind=kLoop, calls=%fused_computation | loop fusion | flops 2096128 | bytes 2101248 | tf_op jit(solution)/shard_map/reduce_sum | solution.py:57
  9.6 0.6 broadcast_in_dim.136
  10.3 3.3 %all-to-all-start.1 = ((f32[4,1,1024]{2,1,0:T(1,128)}), f32[4,1,1024]{2,1,0:T(1,128)S(1)}, u32[]{:S(2)}, u32[]{:S(2)}) async-start(f32[4,1,1024]{2,1,0:T(1,128)} %broadcast_in_dim.136), calls=%async_computation.1 | async-start | bytes 32768 | tf_op jit(solution)/shard_map/all_to_all | solution.py:16
  13.5 0.7 and_compare_fusion.6
  14.2 0.7 broadcast_divide_fusion
  14.9 0.8 constant_dynamic-update-slice_fusion.1
  15.7 0.9 fusion.21
  16.6 0.9 fusion.18
  17.5 0.9 fusion.36
  18.4 0.9 %concatenate.30 = f32[16,1984]{1,0:T(8,128)S(1)} concatenate(f32[16,480]{1,0:T(8,128)S(1)} %collective-permute-done, f32[16,1024]{1,0:T(8,128)} %param.5, f32[16,480]{1,0:T(8,128)S(1)} %collective-permute-done.1), dimensions={1} | concatenate | bytes 253952 | tf_op jit(solution)/shard_map/concatenate | solution.py:25
  19.7 0.2 slice_select_fusion.11
  19.9 0.2 slice_select_fusion.10
  20.2 0.2 slice_select_fusion.9
  20.4 0.2 slice_select_fusion.8
  20.6 0.2 slice_select_fusion.7
  20.9 0.2 slice_select_fusion.6
  21.1 1.0 %copy-done = f32[1024,1024]{1,0:T(8,128)S(1)} copy-done((f32[1024,1024]{1,0:T(8,128)S(1)}, f32[1024,1024]{1,0:T(8,128)}, u32[]{:S(2)}) %copy-start) | copy-done | bytes 4194328
  22.1 3.7 %convolution_bitcast_fusion.2 = f32[8,2,8,128]{3,2,1,0:T(8,128)S(1)} fusion(f32[8,128,1024]{2,1,0:T(8,128)S(1)} %bitcast.133, f32[8,16,1088]{2,1,0:T(8,128)S(1)} %slice_select_fusion.6, pred[8]{0:T(512)(128)(4,1)S(1)} %get-tuple-element.11), kind=kOutput, calls=%fused_computation.3 | convolution fusion | flops 201457664 | bytes 5308928 | tf_op jit(solution)/shard_map/btk,brk->tbr/dot_general | solution.py:42
  25.9 4.5 %collective-permute-start.2 = (f32[16,480]{1,0:T(8,128)S(1)}, f32[16,480]{1,0:T(8,128)S(1)}, u32[]{:S(2)}, u32[]{:S(2)}) collective-permute-start(f32[16,480]{1,0:T(8,128)S(1)} %get-tuple-element.14), channel_id=1, source_target_pairs={{0,4},{4,8},{8,12},{12,16},{16,20},{20,24},{24,28},{1,5},{5,9},{9,... | collective-permute-start | bytes 92168 | tf_op jit(solution)/shard_map/ppermute | solution.py:23
  30.5 6.2 %all_gather.6 = f32[64,1024]{1,0:T(8,128)S(1)} all-gather(f32[16,1024]{1,0:T(8,128)S(1)} %copy-done.3), channel_id=1, replica_groups=mesh['snp'=8,'ind'=4] {'ind'}, dimensions={0}, use_global_device_ids=true | all-gather | bytes 327680 | tf_op jit(solution)/shard_map/all_gather | solution.py:59
  36.8 1.3 %collective-permute-start.3 = (f32[16,480]{1,0:T(8,128)S(1)}, f32[16,480]{1,0:T(8,128)S(1)}, u32[]{:S(2)}, u32[]{:S(2)}) collective-permute-start(f32[16,480]{1,0:T(8,128)S(1)} %get-tuple-element.13), channel_id=1, source_target_pairs={{4,0},{8,4},{12,8},{16,12},{20,16},{24,20},{28,24},{5,1},{9,5},{13... | collective-permute-start | bytes 92168 | tf_op jit(solution)/shard_map/ppermute | solution.py:24
  38.1 4.8 %collective-permute-done.3 = f32[16,480]{1,0:T(8,128)S(1)} collective-permute-done((f32[16,480]{1,0:T(8,128)S(1)}, f32[16,480]{1,0:T(8,128)S(1)}, u32[]{:S(2)}, u32[]{:S(2)}) %collective-permute-start.3) | collective-permute-done | bytes 30752 | tf_op jit(solution)/shard_map/ppermute | solution.py:24
  43.6 0.2 slice_select_fusion.5
  43.8 0.2 slice_select_fusion.4
  44.0 0.2 slice_select_fusion.3
  44.3 0.2 slice_select_fusion.2
  44.5 0.2 slice_select_fusion.1
  44.7 0.2 slice_select_fusion
  45.0 1.0 %copy-done.1 = f32[1024,1024]{1,0:T(8,128)S(1)} copy-done((f32[1024,1024]{1,0:T(8,128)S(1)}, f32[1024,1024]{1,0:T(8,128)}, u32[]{:S(2)}) %copy-start.1) | copy-done | bytes 4194328
  46.0 3.7 %convolution_bitcast_fusion.1 = f32[8,2,8,128]{3,2,1,0:T(8,128)S(1)} fusion(f32[8,128,1024]{2,1,0:T(8,128)S(1)} %bitcast.134, f32[8,16,1088]{2,1,0:T(8,128)S(1)} %slice_select_fusion, pred[8]{0:T(512)(128)(4,1)S(1)} %get-tuple-element.11), kind=kOutput, calls=%fused_computation.2 | convolution fusion | flops 201457664 | bytes 5308928 | tf_op jit(solution)/shard_map/btk,brk->tbr/dot_general | solution.py:42
  49.6 0.2 multiply_reduce_fusion.3
  50.0 0.7 reshape.139
  50.8 6.4 %all-to-all-start = ((f32[32,1,256]{2,1,0:T(1,128)}), f32[32,1,256]{2,1,0:T(1,128)S(1)}, u32[]{:S(2)}, u32[]{:S(2)}) async-start(f32[32,1,256]{2,1,0:T(1,128)} %reshape.139), calls=%async_computation | async-start | bytes 65536 | tf_op jit(solution)/shard_map/all_to_all | solution.py:16
  57.1 6.1 %all_gather.7 = f32[64,1024]{1,0:T(8,128)S(1)} all-gather(f32[16,1024]{1,0:T(8,128)S(1)} %bitcast_add_fusion.1), channel_id=1, replica_groups=mesh['snp'=8,'ind'=4] {'ind'}, dimensions={0}, use_global_device_ids=true | all-gather | bytes 327680 | tf_op jit(solution)/shard_map/all_gather | solution.py:61
  63.3 1.0 %all-to-all-done = f32[32,1,256]{2,1,0:T(1,128)S(1)} async-done(((f32[32,1,256]{2,1,0:T(1,128)}), f32[32,1,256]{2,1,0:T(1,128)S(1)}, u32[]{:S(2)}, u32[]{:S(2)}) %all-to-all-start) | async-done | bytes 32800 | tf_op jit(solution)/shard_map/all_to_all | solution.py:16
  64.3 0.5 broadcast.122
  64.8 0.7 reduce.2
  65.7 0.3 multiply_reduce_fusion
  66.0 0.8 convolution_bitcast_fusion
  66.9 15.1 %all_to_all.22 = f32[8,65,128]{2,1,0:T(8,128)S(1)} all-to-all(f32[8,65,128]{2,1,0:T(8,128)S(1)} %copy.21), channel_id=1, replica_groups=mesh['snp'=8,'ind'=4] {'snp'}, dimensions={0} | all-to-all | bytes 532480 | tf_op jit(solution)/shard_map/all_to_all | solution.py:97
  82.2 0.6 broadcast_in_dim.138
  82.8 2.9 %all-to-all-start.3 = ((f32[32,1,64]{2,1,0:T(1,128)}), f32[32,1,64]{2,1,0:T(1,128)S(1)}, u32[]{:S(2)}, u32[]{:S(2)}) async-start(f32[32,1,64]{2,1,0:T(1,128)} %broadcast_in_dim.138), calls=%async_computation.3 | async-start | bytes 32768 | tf_op jit(solution)/shard_map/all_to_all | solution.py:16
  85.7 0.6 constant_dynamic-slice_fusion
  86.3 6.4 %all-to-all-done.3 = f32[32,1,64]{2,1,0:T(1,128)S(1)} async-done(((f32[32,1,64]{2,1,0:T(1,128)}), f32[32,1,64]{2,1,0:T(1,128)S(1)}, u32[]{:S(2)}, u32[]{:S(2)}) %all-to-all-start.3) | async-done | bytes 8224 | tf_op jit(solution)/shard_map/all_to_all | solution.py:16
  92.8 0.7 fusion.40
  (45 shorter events, 1.8 us)
Async XLA Ops:
  1.5 14.2 %collective-permute-start = (f32[16,480]{1,0:T(8,128)S(1)}, f32[16,480]{1,0:T(8,128)S(1)}, u32[]{:S(2)}, u32[]{:S(2)}) collective-permute-start(f32[16,480]{1,0:T(8,128)S(1)} %get-tuple-element.16), channel_id=1, source_target_pairs={{0,4},{4,8},{8,12},{12,16},{16,20},{20,24},{24,28},{1,5},{5,9},{9,... | collective-permute-start | bytes 92168 | tf_op jit(solution)/shard_map/ppermute | solution.py:23
  6.4 12.0 %collective-permute-start.1 = (f32[16,480]{1,0:T(8,128)S(1)}, f32[16,480]{1,0:T(8,128)S(1)}, u32[]{:S(2)}, u32[]{:S(2)}) collective-permute-start(f32[16,480]{1,0:T(8,128)S(1)} %get-tuple-element.15), channel_id=1, source_target_pairs={{4,0},{8,4},{12,8},{16,12},{20,16},{24,20},{28,24},{5,1},{9,5},{13... | collective-permute-start | bytes 92168 | tf_op jit(solution)/shard_map/ppermute | solution.py:24
  10.3 26.5 %all-to-all-start.1 = ((f32[4,1,1024]{2,1,0:T(1,128)}), f32[4,1,1024]{2,1,0:T(1,128)S(1)}, u32[]{:S(2)}, u32[]{:S(2)}) async-start(f32[4,1,1024]{2,1,0:T(1,128)} %broadcast_in_dim.136), calls=%async_computation.1 | async-start | bytes 32768 | tf_op jit(solution)/shard_map/all_to_all | solution.py:16
  19.9 2.2 %copy-start = (f32[1024,1024]{1,0:T(8,128)S(1)}, f32[1024,1024]{1,0:T(8,128)}, u32[]{:S(2)}) copy-start(f32[1024,1024]{1,0:T(8,128)} %param.6) | copy-start | bytes 12582916
  20.6 5.1 %copy-start.3 = (f32[16,1024]{1,0:T(8,128)S(1)}, f32[16,1024]{1,0:T(8,128)}, u32[]{:S(2)}) copy-start(f32[16,1024]{1,0:T(8,128)} %param.5) | copy-start | bytes 196612
  25.9 12.1 %collective-permute-start.2 = (f32[16,480]{1,0:T(8,128)S(1)}, f32[16,480]{1,0:T(8,128)S(1)}, u32[]{:S(2)}, u32[]{:S(2)}) collective-permute-start(f32[16,480]{1,0:T(8,128)S(1)} %get-tuple-element.14), channel_id=1, source_target_pairs={{0,4},{4,8},{8,12},{12,16},{16,20},{20,24},{24,28},{1,5},{5,9},{9,... | collective-permute-start | bytes 92168 | tf_op jit(solution)/shard_map/ppermute | solution.py:23
  36.8 6.2 %collective-permute-start.3 = (f32[16,480]{1,0:T(8,128)S(1)}, f32[16,480]{1,0:T(8,128)S(1)}, u32[]{:S(2)}, u32[]{:S(2)}) collective-permute-start(f32[16,480]{1,0:T(8,128)S(1)} %get-tuple-element.13), channel_id=1, source_target_pairs={{4,0},{8,4},{12,8},{16,12},{20,16},{24,20},{28,24},{5,1},{9,5},{13... | collective-permute-start | bytes 92168 | tf_op jit(solution)/shard_map/ppermute | solution.py:24
  43.8 2.2 %copy-start.1 = (f32[1024,1024]{1,0:T(8,128)S(1)}, f32[1024,1024]{1,0:T(8,128)}, u32[]{:S(2)}) copy-start(f32[1024,1024]{1,0:T(8,128)} %param.6) | copy-start | bytes 12582916
  44.7 21.3 %copy-start.2 = (bf16[1024,1024]{1,0:T(8,128)(2,1)S(1)}, bf16[1024,1024]{1,0:T(8,128)(2,1)}, u32[]{:S(2)}) copy-start(bf16[1024,1024]{1,0:T(8,128)(2,1)} %param.9) | copy-start | bytes 6291460
  50.8 13.6 %all-to-all-start = ((f32[32,1,256]{2,1,0:T(1,128)}), f32[32,1,256]{2,1,0:T(1,128)S(1)}, u32[]{:S(2)}, u32[]{:S(2)}) async-start(f32[32,1,256]{2,1,0:T(1,128)} %reshape.139), calls=%async_computation | async-start | bytes 65536 | tf_op jit(solution)/shard_map/all_to_all | solution.py:16
  82.8 9.9 %all-to-all-start.3 = ((f32[32,1,64]{2,1,0:T(1,128)}), f32[32,1,64]{2,1,0:T(1,128)S(1)}, u32[]{:S(2)}, u32[]{:S(2)}) async-start(f32[32,1,64]{2,1,0:T(1,128)} %broadcast_in_dim.138), calls=%async_computation.3 | async-start | bytes 32768 | tf_op jit(solution)/shard_map/all_to_all | solution.py:16
where the time goes:
time: 94.3 us; the launch traced here: 93.5 us
  blocking collectives  27.4 us (29%)
  starting transfers between devices  24.5 us (26%)
  waiting for transfers between devices  12.3 us (13%)
  other arithmetic  11.5 us (12%)
  local copies, waits for them, and re-layouts  8.63 us (9%)
  matrix products  8.08 us (9%)
  between operations  1 us (1%)
    all_to_all x1, blocking collectives, local(): lax.all_to_all(sent, 'snp', 0, 0, tiled=True)  15.1 us
    all_to_all x3, starting transfers between devices, all_sum(): return jnp.sum(lax.all_to_all(sent, axes, 0, 0, tiled=True), axis=0)  12.5 us
    ppermute x2, starting transfers between devices, with_halo(): low = lax.ppermute(block[:, block.shape[1] - width:], 'snp', forward)  9.44 us
    all_to_all x3, waiting for transfers between devices, all_sum(): return jnp.sum(lax.all_to_all(sent, axes, 0, 0, tiled=True), axis=0)  7.48 us
    dot_general x2, matrix products, apply_operator(): jnp.einsum('btk,brk->tbr', windows, blocks, precision=lax.Precision.HIGHEST)  7.32 us
    all_gather x1, blocking collectives, local(): beta_all = lax.all_gather(beta_hat, 'ind', axis=0, tiled=True)  6.23 us
    all_gather x1, blocking collectives, local(): image_all = lax.all_gather(image, 'ind', axis=0, tiled=True)  6.14 us
    ppermute x2, waiting for transfers between devices, with_halo(): high = lax.ppermute(block[:, :width], 'snp', backward)  4.84 us
  transfers between devices with their start and end apart: 7, of which 3 were waited for; matrix products, arithmetic and copies ran while one was open for 16% of the time, Pallas kernels for 0%

commit v1 on v0

--- a/solution.py
+++ b/solution.py
@@ -56,9 +56,9 @@
     ridge_shift = M_GENOME / N_GWAS / heritability
     colsum = jnp.sum(genotypes.astype(jnp.float32), axis=0)
     colsum = all_sum(colsum, "ind", n_ind)
-    beta_all = lax.all_gather(beta_hat, "ind", axis=0, tiled=True)
     image = apply_operator(beta_hat, ld_band, shifts, ridge_shift, halo)
-    image_all = lax.all_gather(image, "ind", axis=0, tiled=True)
+    z_new = lax.all_gather(jnp.concatenate([beta_hat, image], 1), "ind", axis=0, tiled=True)
+    beta_all, image_all = jnp.split(z_new, [beta_hat.shape[1]], 1)
     image2 = apply_operator(image, ld_band, shifts, ridge_shift, halo)
     moments = jnp.stack(
         [

time: 94.3 us -> 89.7 us (0.951)
  blocking collectives: 27.4 us -> 23.6 us
  waiting for transfers between devices: 12.3 us -> 11.1 us
    all_gather x2 -> x1, blocking collectives: 12.4 us -> 7.69 us  [local(): lax.all_gather(jnp.concatenate([beta_hat, image], 1), 'ind', axis=0, tile...]
    all_to_all x3, starting transfers between devices: 12.5 us -> 13.8 us  [all_sum(): return jnp.sum(lax.all_to_all(sent, axes, 0, 0, tiled=True), axis=0)]
    all_to_all x3, waiting for transfers between devices: 7.48 us -> 6.43 us  [all_sum(): return jnp.sum(lax.all_to_all(sent, axes, 0, 0, tiled=True), axis=0)]
    ppermute x2, starting transfers between devices: 9.44 us -> 8.47 us  [with_halo(): low = lax.ppermute(block[:, block.shape[1] - width:], 'snp', forward)]
  transfers between devices with their start and end apart: 7 -> 7, of which waited for: 3 -> 3; matrix products, arithmetic and copies ran while one was open for 16% -> 7% of each run, Pallas kernels for 0% -> 0%
where the time goes in v1:
time: 89.7 us; the launch traced here: 88.9 us
  starting transfers between devices  24.9 us (28%)
  blocking collectives  23.6 us (26%)
  other arithmetic  11.5 us (13%)
  waiting for transfers between devices  11.1 us (12%)
  local copies, waits for them, and re-layouts  8.63 us (10%)
  matrix products  8.08 us (9%)
  between operations  1 us (1%)
    all_to_all x1, blocking collectives, local(): lax.all_to_all(sent, 'snp', 0, 0, tiled=True)  16 us
    all_to_all x3, starting transfers between devices, all_sum(): return jnp.sum(lax.all_to_all(sent, axes, 0, 0, tiled=True), axis=0)  13.8 us
    ppermute x2, starting transfers between devices, with_halo(): low = lax.ppermute(block[:, block.shape[1] - width:], 'snp', forward)  8.47 us
    all_gather x1, blocking collectives, local(): lax.all_gather(jnp.concatenate([beta_hat, image], 1), 'ind', axis=0, tile...  7.69 us
    dot_general x2, matrix products, apply_operator(): jnp.einsum('btk,brk->tbr', windows, blocks, precision=lax.Precision.HIGHEST)  7.32 us
    all_to_all x3, waiting for transfers between devices, all_sum(): return jnp.sum(lax.all_to_all(sent, axes, 0, 0, tiled=True), axis=0)  6.43 us
    ppermute x2, waiting for transfers between devices, with_halo(): high = lax.ppermute(block[:, :width], 'snp', backward)  4.42 us
    unnamed x17, local copies, waits for them, and re-layouts  4.02 us
  transfers between devices with their start and end apart: 7, of which 3 were waited for; matrix products, arithmetic and copies ran while one was open for 7% of the time, Pallas kernels for 0%

profile of v1, /device:TPU:0, one launch (start us, length us, event | category | flops | bytes accessed | tf_op | source)
XLA Modules:
  0.0 88.9 jit_solution(13754391755827849297)
XLA Ops:
  0.6 2.0 %convert_reduce_fusion = f32[1024]{0:T(1024)S(1)} fusion(bf16[1024,1024]{1,0:T(8,128)(2,1)} %param.9), kind=kLoop, calls=%fused_computation | loop fusion | flops 2096128 | bytes 2101248 | tf_op jit(solution)/shard_map/reduce_sum | solution.py:57
  2.6 0.6 broadcast_in_dim.136
  3.2 4.2 %all-to-all-start.1 = ((f32[4,1,1024]{2,1,0:T(1,128)}), f32[4,1,1024]{2,1,0:T(1,128)S(1)}, u32[]{:S(2)}, u32[]{:S(2)}) async-start(f32[4,1,1024]{2,1,0:T(1,128)} %broadcast_in_dim.136), calls=%async_computation.1 | async-start | bytes 32768 | tf_op jit(solution)/shard_map/all_to_all | solution.py:16
  7.4 0.8 fusion.51
  8.3 3.9 %collective-permute-start = (f32[16,480]{1,0:T(8,128)S(1)}, f32[16,480]{1,0:T(8,128)S(1)}, u32[]{:S(2)}, u32[]{:S(2)}) collective-permute-start(f32[16,480]{1,0:T(8,128)S(1)} %get-tuple-element.16), channel_id=1, source_target_pairs={{0,4},{4,8},{8,12},{12,16},{16,20},{20,24},{24,28},{1,5},{5,9},{9,... | collective-permute-start | bytes 92168 | tf_op jit(solution)/shard_map/ppermute | solution.py:23
  12.2 1.3 %collective-permute-start.1 = (f32[16,480]{1,0:T(8,128)S(1)}, f32[16,480]{1,0:T(8,128)S(1)}, u32[]{:S(2)}, u32[]{:S(2)}) collective-permute-start(f32[16,480]{1,0:T(8,128)S(1)} %get-tuple-element.15), channel_id=1, source_target_pairs={{4,0},{8,4},{12,8},{16,12},{20,16},{24,20},{28,24},{5,1},{9,5},{13... | collective-permute-start | bytes 92168 | tf_op jit(solution)/shard_map/ppermute | solution.py:24
  13.5 0.7 and_compare_fusion.6
  14.2 0.7 broadcast_divide_fusion
  14.9 0.8 constant_dynamic-update-slice_fusion.1
  15.8 0.9 fusion.25
  16.6 0.9 %fusion.22 = f32[8,16,1151]{2,1,0:T(8,128)S(1)} fusion(f32[8,16,1151]{2,1,0:T(8,128)S(1)} %fusion.25, f32[16,1024]{1,0:T(8,128)} %param.5, f32[16,480]{1,0:T(8,128)S(1)} %collective-permute-done), kind=kLoop, calls=%fused_computation.58 | loop fusion | flops 18416 | bytes 172032
  17.5 0.9 %fusion.40 = f32[8,16,1151]{2,1,0:T(8,128)S(1)} fusion(f32[8,16,1151]{2,1,0:T(8,128)S(1)} %fusion.22, f32[16,1024]{1,0:T(8,128)} %param.5, f32[16,480]{1,0:T(8,128)S(1)} %collective-permute-done), kind=kLoop, calls=%fused_computation.84 | loop fusion | flops 18416 | bytes 172032
  18.5 0.9 %concatenate.33 = f32[16,1984]{1,0:T(8,128)S(1)} concatenate(f32[16,480]{1,0:T(8,128)S(1)} %collective-permute-done, f32[16,1024]{1,0:T(8,128)} %param.5, f32[16,480]{1,0:T(8,128)S(1)} %collective-permute-done.1), dimensions={1} | concatenate | bytes 253952 | tf_op jit(solution)/shard_map/concatenate | solution.py:25
  19.7 0.2 slice_select_fusion.11
  20.0 0.2 slice_select_fusion.10
  20.2 0.2 slice_select_fusion.9
  20.4 0.2 slice_select_fusion.8
  20.7 0.2 slice_select_fusion.7
  20.9 0.2 slice_select_fusion.6
  21.1 1.0 %copy-done = f32[1024,1024]{1,0:T(8,128)S(1)} copy-done((f32[1024,1024]{1,0:T(8,128)S(1)}, f32[1024,1024]{1,0:T(8,128)}, u32[]{:S(2)}) %copy-start) | copy-done | bytes 4194328
  22.2 3.7 %convolution_bitcast_fusion.2 = f32[8,2,8,128]{3,2,1,0:T(8,128)S(1)} fusion(f32[8,128,1024]{2,1,0:T(8,128)S(1)} %bitcast.133, f32[8,16,1088]{2,1,0:T(8,128)S(1)} %slice_select_fusion.6, pred[8]{0:T(512)(128)(4,1)S(1)} %get-tuple-element.11), kind=kOutput, calls=%fused_computation.3 | convolution fusion | flops 201457664 | bytes 5308928 | tf_op jit(solution)/shard_map/btk,brk->tbr/dot_general | solution.py:42
  26.0 4.5 %collective-permute-start.2 = (f32[16,480]{1,0:T(8,128)S(1)}, f32[16,480]{1,0:T(8,128)S(1)}, u32[]{:S(2)}, u32[]{:S(2)}) collective-permute-start(f32[16,480]{1,0:T(8,128)S(1)} %get-tuple-element.14), channel_id=1, source_target_pairs={{0,4},{4,8},{8,12},{12,16},{16,20},{20,24},{24,28},{1,5},{5,9},{9,... | collective-permute-start | bytes 92168 | tf_op jit(solution)/shard_map/ppermute | solution.py:23
  30.5 1.3 %collective-permute-start.3 = (f32[16,480]{1,0:T(8,128)S(1)}, f32[16,480]{1,0:T(8,128)S(1)}, u32[]{:S(2)}, u32[]{:S(2)}) collective-permute-start(f32[16,480]{1,0:T(8,128)S(1)} %get-tuple-element.13), channel_id=1, source_target_pairs={{4,0},{8,4},{12,8},{16,12},{20,16},{24,20},{28,24},{5,1},{9,5},{13... | collective-permute-start | bytes 92168 | tf_op jit(solution)/shard_map/ppermute | solution.py:24
  31.8 0.3 collective-permute-done.2
  32.4 4.4 %collective-permute-done.3 = f32[16,480]{1,0:T(8,128)S(1)} collective-permute-done((f32[16,480]{1,0:T(8,128)S(1)}, f32[16,480]{1,0:T(8,128)S(1)}, u32[]{:S(2)}, u32[]{:S(2)}) %collective-permute-start.3) | collective-permute-done | bytes 30752 | tf_op jit(solution)/shard_map/ppermute | solution.py:24
  37.2 0.2 slice_select_fusion.5
  37.4 0.2 slice_select_fusion.4
  37.7 0.2 slice_select_fusion.3
  37.9 0.2 slice_select_fusion.2
  38.1 0.2 slice_select_fusion.1
  38.4 0.2 slice_select_fusion
  38.6 1.0 %copy-done.1 = f32[1024,1024]{1,0:T(8,128)S(1)} copy-done((f32[1024,1024]{1,0:T(8,128)S(1)}, f32[1024,1024]{1,0:T(8,128)}, u32[]{:S(2)}) %copy-start.1) | copy-done | bytes 4194328
  39.6 3.7 %convolution_bitcast_fusion.1 = f32[8,2,8,128]{3,2,1,0:T(8,128)S(1)} fusion(f32[8,128,1024]{2,1,0:T(8,128)S(1)} %bitcast.134, f32[8,16,1088]{2,1,0:T(8,128)S(1)} %slice_select_fusion, pred[8]{0:T(512)(128)(4,1)S(1)} %get-tuple-element.11), kind=kOutput, calls=%fused_computation.2 | convolution fusion | flops 201457664 | bytes 5308928 | tf_op jit(solution)/shard_map/btk,brk->tbr/dot_general | solution.py:42
  43.3 0.2 multiply_reduce_fusion.3
  43.7 0.7 reshape.139
  44.4 6.8 %all-to-all-start = ((f32[32,1,256]{2,1,0:T(1,128)}), f32[32,1,256]{2,1,0:T(1,128)S(1)}, u32[]{:S(2)}, u32[]{:S(2)}) async-start(f32[32,1,256]{2,1,0:T(1,128)} %reshape.139), calls=%async_computation | async-start | bytes 65536 | tf_op jit(solution)/shard_map/all_to_all | solution.py:16
  51.2 7.7 %all_gather.3 = f32[64,2048]{1,0:T(8,128)S(1)} all-gather(f32[16,2048]{1,0:T(8,128)S(1)} %pad_maximum_fusion), channel_id=1, replica_groups=mesh['snp'=8,'ind'=4] {'ind'}, dimensions={0}, use_global_device_ids=true | all-gather | bytes 655360 | tf_op jit(solution)/shard_map/all_gather | solution.py:60
  58.9 0.5 broadcast.122
  59.4 0.7 reduce.2
  60.3 0.3 multiply_reduce_fusion
  60.6 0.8 convolution_bitcast_fusion
  61.5 16.0 %all_to_all.22 = f32[8,65,128]{2,1,0:T(8,128)S(1)} all-to-all(f32[8,65,128]{2,1,0:T(8,128)S(1)} %copy.21), channel_id=1, replica_groups=mesh['snp'=8,'ind'=4] {'snp'}, dimensions={0} | all-to-all | bytes 532480 | tf_op jit(solution)/shard_map/all_to_all | solution.py:97
  77.5 0.2 multiply_reduce_fusion.4
  77.7 0.6 broadcast_in_dim.138
  78.3 2.8 %all-to-all-start.3 = ((f32[32,1,64]{2,1,0:T(1,128)}), f32[32,1,64]{2,1,0:T(1,128)S(1)}, u32[]{:S(2)}, u32[]{:S(2)}) async-start(f32[32,1,64]{2,1,0:T(1,128)} %broadcast_in_dim.138), calls=%async_computation.3 | async-start | bytes 32768 | tf_op jit(solution)/shard_map/all_to_all | solution.py:16
  81.1 0.6 constant_dynamic-slice_fusion
  81.7 6.4 %all-to-all-done.3 = f32[32,1,64]{2,1,0:T(1,128)S(1)} async-done(((f32[32,1,64]{2,1,0:T(1,128)}), f32[32,1,64]{2,1,0:T(1,128)S(1)}, u32[]{:S(2)}, u32[]{:S(2)}) %all-to-all-start.3) | async-done | bytes 8224 | tf_op jit(solution)/shard_map/all_to_all | solution.py:16
  88.2 0.7 fusion.44
  (45 shorter events, 1.6 us)
Async XLA Ops:
  3.2 12.5 %all-to-all-start.1 = ((f32[4,1,1024]{2,1,0:T(1,128)}), f32[4,1,1024]{2,1,0:T(1,128)S(1)}, u32[]{:S(2)}, u32[]{:S(2)}) async-start(f32[4,1,1024]{2,1,0:T(1,128)} %broadcast_in_dim.136), calls=%async_computation.1 | async-start | bytes 32768 | tf_op jit(solution)/shard_map/all_to_all | solution.py:16
  8.3 7.5 %collective-permute-start = (f32[16,480]{1,0:T(8,128)S(1)}, f32[16,480]{1,0:T(8,128)S(1)}, u32[]{:S(2)}, u32[]{:S(2)}) collective-permute-start(f32[16,480]{1,0:T(8,128)S(1)} %get-tuple-element.16), channel_id=1, source_target_pairs={{0,4},{4,8},{8,12},{12,16},{16,20},{20,24},{24,28},{1,5},{5,9},{9,... | collective-permute-start | bytes 92168 | tf_op jit(solution)/shard_map/ppermute | solution.py:23
  12.2 6.2 %collective-permute-start.1 = (f32[16,480]{1,0:T(8,128)S(1)}, f32[16,480]{1,0:T(8,128)S(1)}, u32[]{:S(2)}, u32[]{:S(2)}) collective-permute-start(f32[16,480]{1,0:T(8,128)S(1)} %get-tuple-element.15), channel_id=1, source_target_pairs={{4,0},{8,4},{12,8},{16,12},{20,16},{24,20},{28,24},{5,1},{9,5},{13... | collective-permute-start | bytes 92168 | tf_op jit(solution)/shard_map/ppermute | solution.py:24
  20.0 2.2 %copy-start = (f32[1024,1024]{1,0:T(8,128)S(1)}, f32[1024,1024]{1,0:T(8,128)}, u32[]{:S(2)}) copy-start(f32[1024,1024]{1,0:T(8,128)} %param.6) | copy-start | bytes 12582916
  20.7 5.1 %copy-start.3 = (f32[16,1024]{1,0:T(8,128)S(1)}, f32[16,1024]{1,0:T(8,128)}, u32[]{:S(2)}) copy-start(f32[16,1024]{1,0:T(8,128)} %param.5) | copy-start | bytes 196612
  26.0 6.1 %collective-permute-start.2 = (f32[16,480]{1,0:T(8,128)S(1)}, f32[16,480]{1,0:T(8,128)S(1)}, u32[]{:S(2)}, u32[]{:S(2)}) collective-permute-start(f32[16,480]{1,0:T(8,128)S(1)} %get-tuple-element.14), channel_id=1, source_target_pairs={{0,4},{4,8},{8,12},{12,16},{16,20},{20,24},{24,28},{1,5},{5,9},{9,... | collective-permute-start | bytes 92168 | tf_op jit(solution)/shard_map/ppermute | solution.py:23
  30.5 6.2 %collective-permute-start.3 = (f32[16,480]{1,0:T(8,128)S(1)}, f32[16,480]{1,0:T(8,128)S(1)}, u32[]{:S(2)}, u32[]{:S(2)}) collective-permute-start(f32[16,480]{1,0:T(8,128)S(1)} %get-tuple-element.13), channel_id=1, source_target_pairs={{4,0},{8,4},{12,8},{16,12},{20,16},{24,20},{28,24},{5,1},{9,5},{13... | collective-permute-start | bytes 92168 | tf_op jit(solution)/shard_map/ppermute | solution.py:24
  37.4 2.2 %copy-start.1 = (f32[1024,1024]{1,0:T(8,128)S(1)}, f32[1024,1024]{1,0:T(8,128)}, u32[]{:S(2)}) copy-start(f32[1024,1024]{1,0:T(8,128)} %param.6) | copy-start | bytes 12582916
  38.3 22.2 %copy-start.2 = (bf16[1024,1024]{1,0:T(8,128)(2,1)S(1)}, bf16[1024,1024]{1,0:T(8,128)(2,1)}, u32[]{:S(2)}) copy-start(bf16[1024,1024]{1,0:T(8,128)(2,1)} %param.9) | copy-start | bytes 6291460
  44.4 14.5 %all-to-all-start = ((f32[32,1,256]{2,1,0:T(1,128)}), f32[32,1,256]{2,1,0:T(1,128)S(1)}, u32[]{:S(2)}, u32[]{:S(2)}) async-start(f32[32,1,256]{2,1,0:T(1,128)} %reshape.139), calls=%async_computation | async-start | bytes 65536 | tf_op jit(solution)/shard_map/all_to_all | solution.py:16
  78.3 9.8 %all-to-all-start.3 = ((f32[32,1,64]{2,1,0:T(1,128)}), f32[32,1,64]{2,1,0:T(1,128)S(1)}, u32[]{:S(2)}, u32[]{:S(2)}) async-start(f32[32,1,64]{2,1,0:T(1,128)} %broadcast_in_dim.138), calls=%async_computation.3 | async-start | bytes 32768 | tf_op jit(solution)/shard_map/all_to_all | solution.py:16
